TPU v7x, 512 devices: a whole 4x4x16 slice. The times are simulated.
512 devices in a mesh: blk: 32 (over z, y_lo), rep: 16 (over x, y_hi, core).
Axes of the slice: x: 4, y: 4 (y_hi: 2, y_lo: 2; y = y_hi * 2 + y_lo), z: 16, core: 2. Of those that a mesh axis runs over, the one named last changes fastest.
Arguments:
- feats: bfloat16 [32768, 256], P(('blk', 'rep')), may hold values from -6 to 6
- weight: bfloat16 [256, 256], replicated, may hold values from -0.375 to 0.375
- bias: float32 [256], replicated, may hold values from -4 to 4
- grad_out: bfloat16 [32768, 256], P(('blk', 'rep')), may hold values from -6 to 6
- tile_values: bfloat16 [32, 16, 2, 64, 128, 128], P('blk', 'rep'), may hold values from -0.03125 to 0.03125
- tile_rows: int32 [32, 16, 2, 64], P('blk', 'rep'), may hold values from 0 to 7, as said below
- tile_cols: int32 [32, 16, 2, 64], P('blk', 'rep'), may hold values from 0 to 7, as said below
- tile_count: int32 [32, 16, 2], P('blk', 'rep'), may hold values from 32 to 64, as said below
Outputs:
- out: bfloat16 [32768, 256], P(('blk', 'rep'))
- grad_feats: bfloat16 [32768, 256], P(('blk', 'rep'))
- grad_weight: float32 [256, 256], P('rep')
- grad_bias: float32 [256], replicated
Inputs may be any that keep to these rules, and one draw needn't show every extreme that they name: `tile_count`: some pair slot of some device holds exactly 64 live entries; slots past the count hold values that must be ignored. Within one pair slot the 64 entries name distinct (tile_rows, tile_cols) cells. `tile_cols`: see tile_rows: cells of one slot are distinct.
All inputs are finite; a program needn't handle non-finite values.
Results may differ from a plain program's by a relative error of at most 0.018.
Values may be sent and summed in bfloat16 or wider, within the bound.
No kernel may reach another device: no remote copies, remote signals or barrier semaphores. Data moves between devices by JAX's collectives and lax.ppermute only.
A program may use at most 64 MiB of HBM per device.

v0:
```python
import jax
import jax.numpy as jnp
from jax import lax
from jax.sharding import PartitionSpec as P


def passed_along(x, axis, by):
    devices = lax.axis_size(axis)
    return lax.ppermute(x, axis, [(i, (i + by) % devices) for i in range(devices)])


def dense_adjacency(tile_vals, tile_row, tile_col, live, tiles_per_part):
    entries, tile_size, _ = tile_vals.shape
    cells = tiles_per_part * tiles_per_part
    cell_of_entry = tile_row * tiles_per_part + tile_col
    alive = jnp.arange(entries) < live
    select = (cell_of_entry[None, :] == jnp.arange(cells)[:, None]) & alive[None, :]
    placed = jnp.dot(
        select.astype(tile_vals.dtype),
        tile_vals.reshape(entries, tile_size * tile_size),
        preferred_element_type=jnp.float32,
    ).astype(tile_vals.dtype)
    placed = placed.reshape(tiles_per_part, tiles_per_part, tile_size, tile_size)
    side = tiles_per_part * tile_size
    return placed.transpose(0, 2, 1, 3).reshape(side, side)


def activation(pre_act, cotangent):
    logistic = jax.nn.sigmoid(pre_act)
    result = (pre_act * logistic).astype(jnp.bfloat16)
    grad_pre = (
        cotangent.astype(jnp.float32) * logistic * (1.0 + pre_act * (1.0 - logistic))
    ).astype(jnp.bfloat16)
    return (result, grad_pre)


def body(feats, weight, bias, grad_out, tile_values, tile_rows, tile_cols, tile_count):
    replicas = lax.axis_size("rep")
    rep_index = lax.axis_index("rep")
    tile_size = tile_values.shape[-1]
    pair_slots = tile_values.shape[2]
    digit_count = (replicas - 1).bit_length()
    values_here = tile_values[0, 0]
    rows_here = tile_rows[0, 0]
    cols_here = tile_cols[0, 0]
    counts_here = tile_count[0, 0]
    hw_slice = jnp.dot(feats, weight, preferred_element_type=jnp.float32).astype(jnp.bfloat16)
    feature_block = lax.all_gather(hw_slice, "rep", axis=0, tiled=True)
    for level in range(digit_count):
        shifted = passed_along(feature_block, "blk", 1 << level)
        feature_block = jnp.where(rep_index // (1 << level) % 2 == 1, shifted, feature_block)
    tiles_per_part = feature_block.shape[0] // tile_size
    adjacency = [
        dense_adjacency(
            values_here[slot], rows_here[slot], cols_here[slot], counts_here[slot], tiles_per_part
        )
        for slot in range(pair_slots)
    ]
    aggregate = jnp.zeros(feature_block.shape, jnp.float32)
    for slot in range(pair_slots):
        aggregate = aggregate + jnp.dot(
            adjacency[slot], feature_block, preferred_element_type=jnp.float32
        )
        if slot + 1 < pair_slots:
            feature_block = passed_along(feature_block, "blk", replicas)
    aggregate_rows = lax.psum_scatter(
        aggregate.astype(jnp.bfloat16), "rep", scatter_dimension=0, tiled=True
    ).astype(jnp.float32)
    out, grad_rows = activation(aggregate_rows + bias, grad_out)
    grad_block = lax.all_gather(grad_rows, "rep", axis=0, tiled=True)
    partial_grad = jnp.zeros(grad_block.shape, jnp.float32)
    for slot in reversed(range(pair_slots)):
        partial_grad = partial_grad + lax.dot_general(
            adjacency[slot],
            grad_block,
            (((0,), (0,)), ((), ())),
            preferred_element_type=jnp.float32,
        )
        if slot > 0:
            partial_grad = passed_along(partial_grad.astype(jnp.bfloat16), "blk", -replicas).astype(
                partial_grad.dtype
            )
    for level in reversed(range(digit_count)):
        shifted = passed_along(partial_grad.astype(jnp.bfloat16), "blk", -(1 << level)).astype(
            partial_grad.dtype
        )
        partial_grad = jnp.where(rep_index // (1 << level) % 2 == 1, shifted, partial_grad)
    grad_hw = lax.psum_scatter(
        partial_grad.astype(jnp.bfloat16), "rep", scatter_dimension=0, tiled=True
    )
    grad_feats = lax.dot_general(
        grad_hw, weight, (((1,), (1,)), ((), ())), preferred_element_type=jnp.float32
    ).astype(jnp.bfloat16)
    weight_terms = lax.dot_general(
        feats, grad_hw, (((0,), (0,)), ((), ())), preferred_element_type=jnp.float32
    )
    weight_rows = weight.shape[0] // replicas
    bias_terms = jnp.sum(grad_rows.astype(jnp.float32), axis=0)
    weight_total, grad_bias = lax.psum((weight_terms, bias_terms), ("blk", "rep"))
    grad_weight = lax.dynamic_slice_in_dim(weight_total, rep_index * weight_rows, weight_rows, 0)
    return (out, grad_feats, grad_weight, grad_bias)


def solution(mesh):
    in_specs = (
        P(("blk", "rep"), None),
        P(),
        P(),
        P(("blk", "rep"), None),
        P("blk", "rep", None, None, None, None),
        P("blk", "rep", None, None),
        P("blk", "rep", None, None),
        P("blk", "rep", None),
    )
    out_specs = (P(("blk", "rep"), None), P(("blk", "rep"), None), P("rep", None), P())
    return jax.shard_map(body, mesh=mesh, in_specs=in_specs, out_specs=out_specs, check_vma=False)
```

profile of v0, /device:TPU:4, one launch (start us, length us, event | category | flops | bytes accessed | tf_op | source)
XLA Modules:
  0.0 1048.3 jit_solution(11181954026101608006)
XLA Ops:
  7.2 0.8 copy-done
  8.1 0.9 convolution_convert_fusion.3
  9.0 22.4 %all_gather.6 = bf16[1024,256]{1,0:T(8,128)(2,1)S(1)} all-gather(bf16[64,256]{1,0:T(8,128)(2,1)S(1)} %convolution_convert_fusion.3), channel_id=1, replica_groups=mesh['blk'=32,'rep'=16] {'rep'}, dimensions={0}, use_global_device_ids=true | all-gather | bytes 557056 | tf_op jit(solution)/shard_map/all_gather | solution.py:48
  31.4 2.1 collective-permute-start
  33.5 21.3 %collective-permute-done = bf16[1024,256]{1,0:T(8,128)(2,1)S(1)} collective-permute-done((bf16[1024,256]{1,0:T(8,128)(2,1)S(1)}, bf16[1024,256]{1,0:T(8,128)(2,1)S(1)}, u32[]{:S(2)}, u32[]{:S(2)}) %collective-permute-start) | collective-permute-done | bytes 524320 | tf_op jit(solution)/shard_map/ppermute | solution.py:9
  54.8 0.1 broadcast_select_fusion
  54.9 1.9 collective-permute-start.1
  56.9 14.7 %collective-permute-done.1 = bf16[1024,256]{1,0:T(8,128)(2,1)S(1)} collective-permute-done((bf16[1024,256]{1,0:T(8,128)(2,1)S(1)}, bf16[1024,256]{1,0:T(8,128)(2,1)S(1)}, u32[]{:S(2)}, u32[]{:S(2)}) %collective-permute-start.1) | collective-permute-done | bytes 524320 | tf_op jit(solution)/shard_map/ppermute | solution.py:9
  71.7 1.9 collective-permute-start.2
  73.7 25.6 %collective-permute-done.2 = bf16[1024,256]{1,0:T(8,128)(2,1)S(1)} collective-permute-done((bf16[1024,256]{1,0:T(8,128)(2,1)S(1)}, bf16[1024,256]{1,0:T(8,128)(2,1)S(1)}, u32[]{:S(2)}, u32[]{:S(2)}) %collective-permute-start.2) | collective-permute-done | bytes 524320 | tf_op jit(solution)/shard_map/ppermute | solution.py:9
  99.4 2.4 collective-permute-start.3
  101.8 0.6 fusion.37
  102.4 0.6 iota_compare_fusion.3
  103.0 2.7 fusion.36
  105.7 41.7 %collective-permute-done.3 = bf16[1024,256]{1,0:T(8,128)(2,1)S(1)} collective-permute-done((bf16[1024,256]{1,0:T(8,128)(2,1)S(1)}, bf16[1024,256]{1,0:T(8,128)(2,1)S(1)}, u32[]{:S(2)}, u32[]{:S(2)}) %collective-permute-start.3) | collective-permute-done | bytes 524320 | tf_op jit(solution)/shard_map/ppermute | solution.py:9
  147.4 0.1 broadcast_select_fusion.3
  147.5 5.2 collective-permute-start.4
  152.7 1.7 convolution_convert_fusion.1
  154.4 0.7 iota_compare_fusion.2
  155.0 1.7 convolution_convert_fusion
  156.7 24.6 %collective-permute-done.4 = bf16[1024,256]{1,0:T(8,128)(2,1)S(1)} collective-permute-done((bf16[1024,256]{1,0:T(8,128)(2,1)S(1)}, bf16[1024,256]{1,0:T(8,128)(2,1)S(1)}, u32[]{:S(2)}, u32[]{:S(2)}) %collective-permute-start.4) | collective-permute-done | bytes 524320 | tf_op jit(solution)/shard_map/ppermute | solution.py:9
  181.4 0.7 fusion.2
  182.1 1.5 fusion.22
  183.7 109.7 %reduce-scatter.3.cloned.1.call-done = bf16[64,256]{1,0:T(8,128)(2,1)} async-done(((bf16[1024,256]{1,0:T(8,128)(2,1)}), bf16[64,256]{1,0:T(8,128)(2,1)}) %reduce-scatter.3.cloned.1.call-update) | async-done | bytes 32784 | tf_op jit(solution)/shard_map/reduce_scatter | solution.py:66
  293.4 1.4 convert_reduce_fusion
  294.9 21.4 %all_gather.7 = bf16[1024,256]{1,0:T(8,128)(2,1)S(1)} all-gather(bf16[64,256]{1,0:T(8,128)(2,1)S(1)} %get-tuple-element.9), channel_id=1, replica_groups=mesh['blk'=32,'rep'=16] {'rep'}, dimensions={0}, use_global_device_ids=true | all-gather | bytes 557056 | tf_op jit(solution)/shard_map/all_gather | solution.py:70
  316.3 2.4 fusion.19
  318.7 12.8 %collective-permute-start.5 = (bf16[1024,256]{1,0:T(8,128)(2,1)S(1)}, bf16[1024,256]{1,0:T(8,128)(2,1)S(1)}, u32[]{:S(2)}, u32[]{:S(2)}) collective-permute-start(bf16[1024,256]{1,0:T(8,128)(2,1)S(1)} %fusion.19), channel_id=1, source_target_pairs={{0,256},{16,272},{32,288},{48,304},{64,320},{80,336},{96,352},{112... | collective-permute-start | bytes 1572872 | tf_op jit(solution)/shard_map/ppermute | solution.py:9
  331.5 25.8 %collective-permute-done.5 = bf16[1024,256]{1,0:T(8,128)(2,1)S(1)} collective-permute-done((bf16[1024,256]{1,0:T(8,128)(2,1)S(1)}, bf16[1024,256]{1,0:T(8,128)(2,1)S(1)}, u32[]{:S(2)}, u32[]{:S(2)}) %collective-permute-start.5) | collective-permute-done | bytes 524320 | tf_op jit(solution)/shard_map/ppermute | solution.py:9
  357.3 0.8 fusion.25
  358.0 17.0 %collective-permute-start.6 = (bf16[1024,256]{1,0:T(8,128)(2,1)S(1)}, bf16[1024,256]{1,0:T(8,128)(2,1)S(1)}, u32[]{:S(2)}, u32[]{:S(2)}) collective-permute-start(bf16[1024,256]{1,0:T(8,128)(2,1)S(1)} %get-tuple-element.17), channel_id=1, source_target_pairs={{0,384},{16,400},{32,416},{48,432},{64,448},{80,464},{96,480},{112... | collective-permute-start | bytes 1572872 | tf_op jit(solution)/shard_map/ppermute | solution.py:9
  375.0 23.2 %collective-permute-done.6 = bf16[1024,256]{1,0:T(8,128)(2,1)S(1)} collective-permute-done((bf16[1024,256]{1,0:T(8,128)(2,1)S(1)}, bf16[1024,256]{1,0:T(8,128)(2,1)S(1)}, u32[]{:S(2)}, u32[]{:S(2)}) %collective-permute-start.6) | collective-permute-done | bytes 524320 | tf_op jit(solution)/shard_map/ppermute | solution.py:9
  398.2 0.2 convert_select_fusion.2
  398.4 25.2 %collective-permute-start.7 = (bf16[1024,256]{1,0:T(8,128)(2,1)S(1)}, bf16[1024,256]{1,0:T(8,128)(2,1)S(1)}, u32[]{:S(2)}, u32[]{:S(2)}) collective-permute-start(bf16[1024,256]{1,0:T(8,128)(2,1)S(1)} %convert_select_fusion.2), channel_id=1, source_target_pairs={{0,448},{16,464},{32,480},{48,496},{64,0},{80,16},{96,32},{112,48}... | collective-permute-start | bytes 1572872 | tf_op jit(solution)/shard_map/ppermute | solution.py:9
  423.7 26.4 %collective-permute-done.7 = bf16[1024,256]{1,0:T(8,128)(2,1)S(1)} collective-permute-done((bf16[1024,256]{1,0:T(8,128)(2,1)S(1)}, bf16[1024,256]{1,0:T(8,128)(2,1)S(1)}, u32[]{:S(2)}, u32[]{:S(2)}) %collective-permute-start.7) | collective-permute-done | bytes 524320 | tf_op jit(solution)/shard_map/ppermute | solution.py:9
  450.0 0.1 fusion.26
  450.2 1.9 collective-permute-start.8
  452.1 13.8 %collective-permute-done.8 = bf16[1024,256]{1,0:T(8,128)(2,1)S(1)} collective-permute-done((bf16[1024,256]{1,0:T(8,128)(2,1)S(1)}, bf16[1024,256]{1,0:T(8,128)(2,1)S(1)}, u32[]{:S(2)}, u32[]{:S(2)}) %collective-permute-start.8) | collective-permute-done | bytes 524320 | tf_op jit(solution)/shard_map/ppermute | solution.py:9
  465.9 0.2 fusion.27
  466.1 3.5 collective-permute-start.9
  469.6 11.4 %collective-permute-done.9 = bf16[1024,256]{1,0:T(8,128)(2,1)S(1)} collective-permute-done((bf16[1024,256]{1,0:T(8,128)(2,1)S(1)}, bf16[1024,256]{1,0:T(8,128)(2,1)S(1)}, u32[]{:S(2)}, u32[]{:S(2)}) %collective-permute-start.9) | collective-permute-done | bytes 524320 | tf_op jit(solution)/shard_map/ppermute | solution.py:9
  481.0 1.0 select_convert_fusion
  482.1 106.1 %psum.15 = f32[256]{0:T(256)} all-reduce(f32[256]{0:T(256)S(1)} %get-tuple-element.8), channel_id=1, replica_groups=mesh['blk'=32,'rep'=16] {'blk','rep'}, use_global_device_ids=true, to_apply=%region_4.5 | all-reduce | flops 256 | bytes 2048 | tf_op jit(solution)/shard_map/psum | solution.py:99
  588.2 1.7 convolution_bitcast_fusion
  589.9 1.6 convolution_convert_fusion.2
  591.4 448.7 %all-reduce.2.cloned.1.call-done = f32[256,256]{0,1:T(8,128)} async-done(((f32[256,256]{0,1:T(8,128)}), f32[256,256]{0,1:T(8,128)}) %all-reduce.2.cloned.1.call-update) | async-done | bytes 262160 | tf_op jit(solution)/shard_map/psum | solution.py:99
  1040.1 1.0 constant_dynamic-slice_fusion
  1041.1 0.7 copy.12
  (25 shorter events, 0.3 us)
Async XLA Ops:
  7.2 0.9 copy-start
  7.2 66.4 %copy-start.6 = (s32[1,1,2,64]{3,2,1,0:T(2,128)S(1)}, s32[1,1,2,64]{3,2,1,0:T(2,128)}, u32[]{:S(2)}) copy-start(s32[1,1,2,64]{3,2,1,0:T(2,128)} %param.14) | copy-start | bytes 1540
  7.2 66.4 %copy-start.7 = (s32[1,1,2,64]{3,2,1,0:T(2,128)S(1)}, s32[1,1,2,64]{3,2,1,0:T(2,128)}, u32[]{:S(2)}) copy-start(s32[1,1,2,64]{3,2,1,0:T(2,128)} %param.13) | copy-start | bytes 1540
  7.2 286.2 %reduce-scatter.3.cloned.1.call-start = ((), (), s32[]{:S(2)}) async-start(), calls=%async_computation.2 | async-start | bytes 557056 | tf_op jit(solution)/shard_map/reduce_scatter | solution.py:66
  31.4 23.5 %collective-permute-start = (bf16[1024,256]{1,0:T(8,128)(2,1)S(1)}, bf16[1024,256]{1,0:T(8,128)(2,1)S(1)}, u32[]{:S(2)}, u32[]{:S(2)}) collective-permute-start(bf16[1024,256]{1,0:T(8,128)(2,1)S(1)} %all_gather.6), channel_id=1, source_target_pairs={{0,16},{16,32},{32,48},{48,64},{64,80},{80,96},{96,112},{112,128},... | collective-permute-start | bytes 1572872 | tf_op jit(solution)/shard_map/ppermute | solution.py:9
  33.5 68.3 %copy-start.4 = (s32[1,1,2]{2,1,0:T(1,128)S(1)}, s32[1,1,2]{2,1,0:T(1,128)}, u32[]{:S(2)}) copy-start(s32[1,1,2]{2,1,0:T(1,128)} %param.15) | copy-start | bytes 28
  54.9 16.7 %collective-permute-start.1 = (bf16[1024,256]{1,0:T(8,128)(2,1)S(1)}, bf16[1024,256]{1,0:T(8,128)(2,1)S(1)}, u32[]{:S(2)}, u32[]{:S(2)}) collective-permute-start(bf16[1024,256]{1,0:T(8,128)(2,1)S(1)} %broadcast_select_fusion), channel_id=1, source_target_pairs={{0,32},{16,48},{32,64},{48,80},{64,96},{80,112},{96,128},{112,144}... | collective-permute-start | bytes 1572872 | tf_op jit(solution)/shard_map/ppermute | solution.py:9
  71.7 27.6 %collective-permute-start.2 = (bf16[1024,256]{1,0:T(8,128)(2,1)S(1)}, bf16[1024,256]{1,0:T(8,128)(2,1)S(1)}, u32[]{:S(2)}, u32[]{:S(2)}) collective-permute-start(bf16[1024,256]{1,0:T(8,128)(2,1)S(1)} %broadcast_select_fusion.1), channel_id=1, source_target_pairs={{0,64},{16,80},{32,96},{48,112},{64,128},{80,144},{96,160},{112,17... | collective-permute-start | bytes 1572872 | tf_op jit(solution)/shard_map/ppermute | solution.py:9
  99.4 48.1 %collective-permute-start.3 = (bf16[1024,256]{1,0:T(8,128)(2,1)S(1)}, bf16[1024,256]{1,0:T(8,128)(2,1)S(1)}, u32[]{:S(2)}, u32[]{:S(2)}) collective-permute-start(bf16[1024,256]{1,0:T(8,128)(2,1)S(1)} %broadcast_select_fusion.2), channel_id=1, source_target_pairs={{0,128},{16,144},{32,160},{48,176},{64,192},{80,208},{96,224},{112... | collective-permute-start | bytes 1572872 | tf_op jit(solution)/shard_map/ppermute | solution.py:9
  147.5 33.9 %collective-permute-start.4 = (bf16[1024,256]{1,0:T(8,128)(2,1)S(1)}, bf16[1024,256]{1,0:T(8,128)(2,1)S(1)}, u32[]{:S(2)}, u32[]{:S(2)}) collective-permute-start(bf16[1024,256]{1,0:T(8,128)(2,1)S(1)} %broadcast_select_fusion.3), channel_id=1, source_target_pairs={{0,256},{16,272},{32,288},{48,304},{64,320},{80,336},{96,352},{112... | collective-permute-start | bytes 1572872 | tf_op jit(solution)/shard_map/ppermute | solution.py:9
  156.7 25.3 %copy-start.1 = (bf16[64,16384]{1,0:T(8,128)(2,1)}, bf16[64,16384]{1,0:T(8,128)(2,1)S(1)}, u32[]{:S(2)}) copy-start(bf16[64,16384]{1,0:T(8,128)(2,1)S(1)} %convolution_convert_fusion) | copy-start | bytes 6291460
  182.1 111.4 %copy-start.3 = (bf16[64,256]{1,0:T(8,128)(2,1)S(1)}, bf16[64,256]{1,0:T(8,128)(2,1)}, u32[]{:S(2)}) copy-start(bf16[64,256]{1,0:T(8,128)(2,1)} %param.11) | copy-start | bytes 98308
  182.1 111.3 %copy-start.5 = (f32[256]{0:T(256)S(1)}, f32[256]{0:T(256)}, u32[]{:S(2)}) copy-start(f32[256]{0:T(256)} %param.10) | copy-start | bytes 3076
  183.7 404.5 %reduce-scatter.5.cloned.1.call-start = ((), (), s32[]{:S(2)}) async-start(), calls=%async_computation.3 | async-start | bytes 557056 | tf_op jit(solution)/shard_map/reduce_scatter | solution.py:88
  318.7 38.6 %collective-permute-start.5 = (bf16[1024,256]{1,0:T(8,128)(2,1)S(1)}, bf16[1024,256]{1,0:T(8,128)(2,1)S(1)}, u32[]{:S(2)}, u32[]{:S(2)}) collective-permute-start(bf16[1024,256]{1,0:T(8,128)(2,1)S(1)} %fusion.19), channel_id=1, source_target_pairs={{0,256},{16,272},{32,288},{48,304},{64,320},{80,336},{96,352},{112... | collective-permute-start | bytes 1572872 | tf_op jit(solution)/shard_map/ppermute | solution.py:9
  358.0 40.2 %collective-permute-start.6 = (bf16[1024,256]{1,0:T(8,128)(2,1)S(1)}, bf16[1024,256]{1,0:T(8,128)(2,1)S(1)}, u32[]{:S(2)}, u32[]{:S(2)}) collective-permute-start(bf16[1024,256]{1,0:T(8,128)(2,1)S(1)} %get-tuple-element.17), channel_id=1, source_target_pairs={{0,384},{16,400},{32,416},{48,432},{64,448},{80,464},{96,480},{112... | collective-permute-start | bytes 1572872 | tf_op jit(solution)/shard_map/ppermute | solution.py:9
  398.4 51.6 %collective-permute-start.7 = (bf16[1024,256]{1,0:T(8,128)(2,1)S(1)}, bf16[1024,256]{1,0:T(8,128)(2,1)S(1)}, u32[]{:S(2)}, u32[]{:S(2)}) collective-permute-start(bf16[1024,256]{1,0:T(8,128)(2,1)S(1)} %convert_select_fusion.2), channel_id=1, source_target_pairs={{0,448},{16,464},{32,480},{48,496},{64,0},{80,16},{96,32},{112,48}... | collective-permute-start | bytes 1572872 | tf_op jit(solution)/shard_map/ppermute | solution.py:9
  450.2 15.7 %collective-permute-start.8 = (bf16[1024,256]{1,0:T(8,128)(2,1)S(1)}, bf16[1024,256]{1,0:T(8,128)(2,1)S(1)}, u32[]{:S(2)}, u32[]{:S(2)}) collective-permute-start(bf16[1024,256]{1,0:T(8,128)(2,1)S(1)} %fusion.26), channel_id=1, source_target_pairs={{0,480},{16,496},{32,0},{48,16},{64,32},{80,48},{96,64},{112,80},{... | collective-permute-start | bytes 1572872 | tf_op jit(solution)/shard_map/ppermute | solution.py:9
  466.1 122.1 %copy-start.2 = (bf16[64,256]{1,0:T(8,128)(2,1)S(1)}, bf16[64,256]{1,0:T(8,128)(2,1)}, u32[]{:S(2)}) copy-start(bf16[64,256]{1,0:T(8,128)(2,1)} %param.8) | copy-start | bytes 98308
  466.1 14.9 %collective-permute-start.9 = (bf16[1024,256]{1,0:T(8,128)(2,1)S(1)}, bf16[1024,256]{1,0:T(8,128)(2,1)S(1)}, u32[]{:S(2)}, u32[]{:S(2)}) collective-permute-start(bf16[1024,256]{1,0:T(8,128)(2,1)S(1)} %fusion.27), channel_id=1, source_target_pairs={{0,496},{16,0},{32,16},{48,32},{64,48},{80,64},{96,80},{112,96},{1... | collective-permute-start | bytes 1572872 | tf_op jit(solution)/shard_map/ppermute | solution.py:9
  482.1 558.0 %all-reduce.2.cloned.1.call-start = ((), (), s32[]{:S(2)}) async-start(), calls=%async_computation.4 | async-start | bytes 524288 | tf_op jit(solution)/shard_map/psum | solution.py:99
Sparse Core Ops, SparseCore 0:
  183.8 109.6 reduce-scatter.2
  482.2 85.5 reduce-scatter.4
  590.0 450.0 all-reduce.1
where the time goes:
time: 1050 us
  waiting for transfers between devices  787 us (75%)
  blocking collectives  150 us (14%)
  starting transfers between devices  74 us (7%)
  between operations  14.1 us (1%)
  matrix products  12.9 us (1%)
    psum x1, waiting for transfers between devices, body(): lax.psum((weight_terms, bias_terms), ('blk', 'rep'))  449 us
    ppermute x10, waiting for transfers between devices, passed_along(): lax.ppermute(x, axis, [(i, (i + by) % devices) for i in range(devices)])  229 us
    reduce_scatter x1, waiting for transfers between devices, body(): lax.psum_scatter(aggregate.astype(jnp.bfloat16), 'rep', scatter_dimension...  110 us
    psum x1, blocking collectives, body(): lax.psum((weight_terms, bias_terms), ('blk', 'rep'))  106 us
    ppermute x10, starting transfers between devices, passed_along(): lax.ppermute(x, axis, [(i, (i + by) % devices) for i in range(devices)])  73.9 us
    all_gather x1, blocking collectives, body(): feature_block = lax.all_gather(hw_slice, 'rep', axis=0, tiled=True)  22.4 us
    all_gather x1, blocking collectives, body(): grad_block = lax.all_gather(grad_rows, 'rep', axis=0, tiled=True)  21.4 us
  transfers between devices with their start and end apart: 13, of which 12 were waited for; matrix products, arithmetic and copies ran while one was open for 1% of the time, Pallas kernels for 0%

commit v1 on v0

--- a/solution.py
+++ b/solution.py
@@ -96,7 +96,7 @@
     )
     weight_rows = weight.shape[0] // replicas
     bias_terms = jnp.sum(grad_rows.astype(jnp.float32), axis=0)
-    weight_total, grad_bias = lax.psum((weight_terms, bias_terms), ("blk", "rep"))
+    weight_total, grad_bias = lax.psum(lax.psum((weight_terms, bias_terms), "rep"), "blk")
     grad_weight = lax.dynamic_slice_in_dim(weight_total, rep_index * weight_rows, weight_rows, 0)
     return (out, grad_feats, grad_weight, grad_bias)
 

time: 1050 us -> 998 us (0.950)
  the two profiles are of different devices: /device:TPU:4 before, /device:TPU:2 now
where the time goes in v1:
time: 998 us; the launch traced here: 997 us
  waiting for transfers between devices  737 us (74%)
  blocking collectives  146 us (15%)
  starting transfers between devices  77.3 us (8%)
  between operations  14.1 us (1%)
  matrix products  12.9 us (1%)
    ppermute x10, waiting for transfers between devices, passed_along(): lax.ppermute(x, axis, [(i, (i + by) % devices) for i in range(devices)])  237 us
    psum x1, waiting for transfers between devices, body(): lax.psum(lax.psum((weight_terms, bias_terms), 'rep'), 'blk')  169 us
    psum x1, waiting for transfers between devices, body(): lax.psum((weight_terms, bias_terms), 'rep')  147 us
    reduce_scatter x1, waiting for transfers between devices, body(): lax.psum_scatter(aggregate.astype(jnp.bfloat16), 'rep', scatter_dimension...  97.9 us
    reduce_scatter x1, waiting for transfers between devices, body(): lax.psum_scatter(partial_grad.astype(jnp.bfloat16), 'rep', scatter_dimens...  85.5 us
    ppermute x10, starting transfers between devices, passed_along(): lax.ppermute(x, axis, [(i, (i + by) % devices) for i in range(devices)])  77.1 us
    psum x1, blocking collectives, body(): lax.psum(lax.psum((weight_terms, bias_terms), 'rep'), 'blk')  64.6 us
    psum x1, blocking collectives, body(): lax.psum((weight_terms, bias_terms), 'rep')  36.2 us
  transfers between devices with their start and end apart: 14, of which 14 were waited for; matrix products, arithmetic and copies ran while one was open for 1% of the time, Pallas kernels for 0%

profile of v1, /device:TPU:2, one launch (start us, length us, event | category | flops | bytes accessed | tf_op | source)
XLA Modules:
  0.0 997.0 jit_solution(9610833215569753904)
XLA Ops:
  7.2 0.8 copy-done
  8.1 0.9 convolution_convert_fusion.3
  9.0 23.8 %all_gather.6 = bf16[1024,256]{1,0:T(8,128)(2,1)S(1)} all-gather(bf16[64,256]{1,0:T(8,128)(2,1)S(1)} %convolution_convert_fusion.3), channel_id=1, replica_groups=mesh['blk'=32,'rep'=16] {'rep'}, dimensions={0}, use_global_device_ids=true | all-gather | bytes 557056 | tf_op jit(solution)/shard_map/all_gather | solution.py:48
  32.7 2.5 collective-permute-start
  35.3 21.3 %collective-permute-done = bf16[1024,256]{1,0:T(8,128)(2,1)S(1)} collective-permute-done((bf16[1024,256]{1,0:T(8,128)(2,1)S(1)}, bf16[1024,256]{1,0:T(8,128)(2,1)S(1)}, u32[]{:S(2)}, u32[]{:S(2)}) %collective-permute-start) | collective-permute-done | bytes 524320 | tf_op jit(solution)/shard_map/ppermute | solution.py:9
  56.7 1.9 collective-permute-start.1
  58.6 14.7 %collective-permute-done.1 = bf16[1024,256]{1,0:T(8,128)(2,1)S(1)} collective-permute-done((bf16[1024,256]{1,0:T(8,128)(2,1)S(1)}, bf16[1024,256]{1,0:T(8,128)(2,1)S(1)}, u32[]{:S(2)}, u32[]{:S(2)}) %collective-permute-start.1) | collective-permute-done | bytes 524320 | tf_op jit(solution)/shard_map/ppermute | solution.py:9
  73.4 1.9 collective-permute-start.2
  75.4 25.2 %collective-permute-done.2 = bf16[1024,256]{1,0:T(8,128)(2,1)S(1)} collective-permute-done((bf16[1024,256]{1,0:T(8,128)(2,1)S(1)}, bf16[1024,256]{1,0:T(8,128)(2,1)S(1)}, u32[]{:S(2)}, u32[]{:S(2)}) %collective-permute-start.2) | collective-permute-done | bytes 524320 | tf_op jit(solution)/shard_map/ppermute | solution.py:9
  100.7 2.9 collective-permute-start.3
  103.7 0.6 fusion.37
  104.2 0.6 iota_compare_fusion.3
  104.9 2.7 fusion.36
  107.6 39.3 %collective-permute-done.3 = bf16[1024,256]{1,0:T(8,128)(2,1)S(1)} collective-permute-done((bf16[1024,256]{1,0:T(8,128)(2,1)S(1)}, bf16[1024,256]{1,0:T(8,128)(2,1)S(1)}, u32[]{:S(2)}, u32[]{:S(2)}) %collective-permute-start.3) | collective-permute-done | bytes 524320 | tf_op jit(solution)/shard_map/ppermute | solution.py:9
  147.0 5.7 collective-permute-start.4
  152.7 1.7 convolution_convert_fusion.1
  154.4 0.7 iota_compare_fusion.2
  155.1 1.7 convolution_convert_fusion
  156.8 37.7 %collective-permute-done.4 = bf16[1024,256]{1,0:T(8,128)(2,1)S(1)} collective-permute-done((bf16[1024,256]{1,0:T(8,128)(2,1)S(1)}, bf16[1024,256]{1,0:T(8,128)(2,1)S(1)}, u32[]{:S(2)}, u32[]{:S(2)}) %collective-permute-start.4) | collective-permute-done | bytes 524320 | tf_op jit(solution)/shard_map/ppermute | solution.py:9
  194.5 0.7 fusion.2
  195.2 1.5 fusion.22
  196.8 97.9 %reduce-scatter.3.cloned.1.call-done = bf16[64,256]{1,0:T(8,128)(2,1)} async-done(((bf16[1024,256]{1,0:T(8,128)(2,1)}), bf16[64,256]{1,0:T(8,128)(2,1)}) %reduce-scatter.3.cloned.1.call-update) | async-done | bytes 32784 | tf_op jit(solution)/shard_map/reduce_scatter | solution.py:66
  294.7 1.4 convert_reduce_fusion
  296.1 21.2 %all_gather.7 = bf16[1024,256]{1,0:T(8,128)(2,1)S(1)} all-gather(bf16[64,256]{1,0:T(8,128)(2,1)S(1)} %get-tuple-element.9), channel_id=1, replica_groups=mesh['blk'=32,'rep'=16] {'rep'}, dimensions={0}, use_global_device_ids=true | all-gather | bytes 557056 | tf_op jit(solution)/shard_map/all_gather | solution.py:70
  317.3 2.4 fusion.19
  319.7 12.8 %collective-permute-start.5 = (bf16[1024,256]{1,0:T(8,128)(2,1)S(1)}, bf16[1024,256]{1,0:T(8,128)(2,1)S(1)}, u32[]{:S(2)}, u32[]{:S(2)}) collective-permute-start(bf16[1024,256]{1,0:T(8,128)(2,1)S(1)} %fusion.19), channel_id=1, source_target_pairs={{0,256},{16,272},{32,288},{48,304},{64,320},{80,336},{96,352},{112... | collective-permute-start | bytes 1572872 | tf_op jit(solution)/shard_map/ppermute | solution.py:9
  332.4 25.8 %collective-permute-done.5 = bf16[1024,256]{1,0:T(8,128)(2,1)S(1)} collective-permute-done((bf16[1024,256]{1,0:T(8,128)(2,1)S(1)}, bf16[1024,256]{1,0:T(8,128)(2,1)S(1)}, u32[]{:S(2)}, u32[]{:S(2)}) %collective-permute-start.5) | collective-permute-done | bytes 524320 | tf_op jit(solution)/shard_map/ppermute | solution.py:9
  358.2 0.8 fusion.25
  359.0 17.2 %collective-permute-start.6 = (bf16[1024,256]{1,0:T(8,128)(2,1)S(1)}, bf16[1024,256]{1,0:T(8,128)(2,1)S(1)}, u32[]{:S(2)}, u32[]{:S(2)}) collective-permute-start(bf16[1024,256]{1,0:T(8,128)(2,1)S(1)} %get-tuple-element.17), channel_id=1, source_target_pairs={{0,384},{16,400},{32,416},{48,432},{64,448},{80,464},{96,480},{112... | collective-permute-start | bytes 1572872 | tf_op jit(solution)/shard_map/ppermute | solution.py:9
  376.2 23.5 %collective-permute-done.6 = bf16[1024,256]{1,0:T(8,128)(2,1)S(1)} collective-permute-done((bf16[1024,256]{1,0:T(8,128)(2,1)S(1)}, bf16[1024,256]{1,0:T(8,128)(2,1)S(1)}, u32[]{:S(2)}, u32[]{:S(2)}) %collective-permute-start.6) | collective-permute-done | bytes 524320 | tf_op jit(solution)/shard_map/ppermute | solution.py:9
  399.7 0.2 convert_select_fusion.2
  399.9 26.3 %collective-permute-start.7 = (bf16[1024,256]{1,0:T(8,128)(2,1)S(1)}, bf16[1024,256]{1,0:T(8,128)(2,1)S(1)}, u32[]{:S(2)}, u32[]{:S(2)}) collective-permute-start(bf16[1024,256]{1,0:T(8,128)(2,1)S(1)} %convert_select_fusion.2), channel_id=1, source_target_pairs={{0,448},{16,464},{32,480},{48,496},{64,0},{80,16},{96,32},{112,48}... | collective-permute-start | bytes 1572872 | tf_op jit(solution)/shard_map/ppermute | solution.py:9
  426.2 24.9 %collective-permute-done.7 = bf16[1024,256]{1,0:T(8,128)(2,1)S(1)} collective-permute-done((bf16[1024,256]{1,0:T(8,128)(2,1)S(1)}, bf16[1024,256]{1,0:T(8,128)(2,1)S(1)}, u32[]{:S(2)}, u32[]{:S(2)}) %collective-permute-start.7) | collective-permute-done | bytes 524320 | tf_op jit(solution)/shard_map/ppermute | solution.py:9
  451.2 1.9 collective-permute-start.8
  453.1 13.8 %collective-permute-done.8 = bf16[1024,256]{1,0:T(8,128)(2,1)S(1)} collective-permute-done((bf16[1024,256]{1,0:T(8,128)(2,1)S(1)}, bf16[1024,256]{1,0:T(8,128)(2,1)S(1)}, u32[]{:S(2)}, u32[]{:S(2)}) %collective-permute-start.8) | collective-permute-done | bytes 524320 | tf_op jit(solution)/shard_map/ppermute | solution.py:9
  466.9 0.2 fusion.27
  467.1 4.0 collective-permute-start.9
  471.1 10.9 %collective-permute-done.9 = bf16[1024,256]{1,0:T(8,128)(2,1)S(1)} collective-permute-done((bf16[1024,256]{1,0:T(8,128)(2,1)S(1)}, bf16[1024,256]{1,0:T(8,128)(2,1)S(1)}, u32[]{:S(2)}, u32[]{:S(2)}) %collective-permute-start.9) | collective-permute-done | bytes 524320 | tf_op jit(solution)/shard_map/ppermute | solution.py:9
  482.0 1.0 select_convert_fusion
  483.1 85.5 %reduce-scatter.5.cloned.1.call-done = bf16[64,256]{1,0:T(8,128)(2,1)} async-done(((bf16[1024,256]{1,0:T(8,128)(2,1)}), bf16[64,256]{1,0:T(8,128)(2,1)}) %reduce-scatter.5.cloned.1.call-update) | async-done | bytes 32784 | tf_op jit(solution)/shard_map/reduce_scatter | solution.py:88
  568.6 1.7 convolution_bitcast_fusion
  570.4 147.3 %all-reduce.3.cloned.1.call-done = f32[256,256]{0,1:T(8,128)} async-done(((f32[256,256]{0,1:T(8,128)}), f32[256,256]{0,1:T(8,128)}) %all-reduce.3.cloned.1.call-update) | async-done | bytes 262160 | tf_op jit(solution)/shard_map/psum | solution.py:99
  717.6 36.2 %psum.30 = f32[256]{0:T(256)S(1)} all-reduce(f32[256]{0:T(256)S(1)} %get-tuple-element.8), channel_id=1, replica_groups=mesh['blk'=32,'rep'=16] {'rep'}, use_global_device_ids=true, to_apply=%region_5.6 | all-reduce | flops 256 | bytes 2048 | tf_op jit(solution)/shard_map/psum | solution.py:99
  753.8 64.6 %psum.31 = f32[256]{0:T(256)} all-reduce(f32[256]{0:T(256)S(1)} %psum.30), channel_id=1, replica_groups=mesh['blk'=32,'rep'=16] {'blk'}, use_global_device_ids=true, to_apply=%region_6.7 | all-reduce | flops 256 | bytes 2048 | tf_op jit(solution)/shard_map/psum | solution.py:99
  818.4 1.6 convolution_convert_fusion.2
  819.9 168.8 %all-reduce.5.cloned.1.call-done = f32[256,256]{0,1:T(8,128)} async-done(((f32[256,256]{0,1:T(8,128)}), f32[256,256]{0,1:T(8,128)}) %all-reduce.5.cloned.1.call-update) | async-done | bytes 262160 | tf_op jit(solution)/shard_map/psum | solution.py:99
  988.8 1.0 constant_dynamic-slice_fusion
  989.8 0.7 copy.12
  (29 shorter events, 0.6 us)
Async XLA Ops:
  7.2 0.9 copy-start
  7.2 68.2 %copy-start.6 = (s32[1,1,2,64]{3,2,1,0:T(2,128)S(1)}, s32[1,1,2,64]{3,2,1,0:T(2,128)}, u32[]{:S(2)}) copy-start(s32[1,1,2,64]{3,2,1,0:T(2,128)} %param.14) | copy-start | bytes 1540
  7.2 68.2 %copy-start.7 = (s32[1,1,2,64]{3,2,1,0:T(2,128)S(1)}, s32[1,1,2,64]{3,2,1,0:T(2,128)}, u32[]{:S(2)}) copy-start(s32[1,1,2,64]{3,2,1,0:T(2,128)} %param.13) | copy-start | bytes 1540
  7.2 287.5 %reduce-scatter.3.cloned.1.call-start = ((), (), s32[]{:S(2)}) async-start(), calls=%async_computation.2 | async-start | bytes 557056 | tf_op jit(solution)/shard_map/reduce_scatter | solution.py:66
  32.7 23.9 %collective-permute-start = (bf16[1024,256]{1,0:T(8,128)(2,1)S(1)}, bf16[1024,256]{1,0:T(8,128)(2,1)S(1)}, u32[]{:S(2)}, u32[]{:S(2)}) collective-permute-start(bf16[1024,256]{1,0:T(8,128)(2,1)S(1)} %all_gather.6), channel_id=1, source_target_pairs={{0,16},{16,32},{32,48},{48,64},{64,80},{80,96},{96,112},{112,128},... | collective-permute-start | bytes 1572872 | tf_op jit(solution)/shard_map/ppermute | solution.py:9
  35.3 68.4 %copy-start.4 = (s32[1,1,2]{2,1,0:T(1,128)S(1)}, s32[1,1,2]{2,1,0:T(1,128)}, u32[]{:S(2)}) copy-start(s32[1,1,2]{2,1,0:T(1,128)} %param.15) | copy-start | bytes 28
  56.7 16.7 %collective-permute-start.1 = (bf16[1024,256]{1,0:T(8,128)(2,1)S(1)}, bf16[1024,256]{1,0:T(8,128)(2,1)S(1)}, u32[]{:S(2)}, u32[]{:S(2)}) collective-permute-start(bf16[1024,256]{1,0:T(8,128)(2,1)S(1)} %broadcast_select_fusion), channel_id=1, source_target_pairs={{0,32},{16,48},{32,64},{48,80},{64,96},{80,112},{96,128},{112,144}... | collective-permute-start | bytes 1572872 | tf_op jit(solution)/shard_map/ppermute | solution.py:9
  73.4 27.2 %collective-permute-start.2 = (bf16[1024,256]{1,0:T(8,128)(2,1)S(1)}, bf16[1024,256]{1,0:T(8,128)(2,1)S(1)}, u32[]{:S(2)}, u32[]{:S(2)}) collective-permute-start(bf16[1024,256]{1,0:T(8,128)(2,1)S(1)} %broadcast_select_fusion.1), channel_id=1, source_target_pairs={{0,64},{16,80},{32,96},{48,112},{64,128},{80,144},{96,160},{112,17... | collective-permute-start | bytes 1572872 | tf_op jit(solution)/shard_map/ppermute | solution.py:9
  100.7 46.3 %collective-permute-start.3 = (bf16[1024,256]{1,0:T(8,128)(2,1)S(1)}, bf16[1024,256]{1,0:T(8,128)(2,1)S(1)}, u32[]{:S(2)}, u32[]{:S(2)}) collective-permute-start(bf16[1024,256]{1,0:T(8,128)(2,1)S(1)} %broadcast_select_fusion.2), channel_id=1, source_target_pairs={{0,128},{16,144},{32,160},{48,176},{64,192},{80,208},{96,224},{112... | collective-permute-start | bytes 1572872 | tf_op jit(solution)/shard_map/ppermute | solution.py:9
  147.0 47.4 %collective-permute-start.4 = (bf16[1024,256]{1,0:T(8,128)(2,1)S(1)}, bf16[1024,256]{1,0:T(8,128)(2,1)S(1)}, u32[]{:S(2)}, u32[]{:S(2)}) collective-permute-start(bf16[1024,256]{1,0:T(8,128)(2,1)S(1)} %broadcast_select_fusion.3), channel_id=1, source_target_pairs={{0,256},{16,272},{32,288},{48,304},{64,320},{80,336},{96,352},{112... | collective-permute-start | bytes 1572872 | tf_op jit(solution)/shard_map/ppermute | solution.py:9
  156.8 38.4 %copy-start.1 = (bf16[64,16384]{1,0:T(8,128)(2,1)}, bf16[64,16384]{1,0:T(8,128)(2,1)S(1)}, u32[]{:S(2)}) copy-start(bf16[64,16384]{1,0:T(8,128)(2,1)S(1)} %convolution_convert_fusion) | copy-start | bytes 6291460
  195.2 99.5 %copy-start.3 = (bf16[64,256]{1,0:T(8,128)(2,1)S(1)}, bf16[64,256]{1,0:T(8,128)(2,1)}, u32[]{:S(2)}) copy-start(bf16[64,256]{1,0:T(8,128)(2,1)} %param.11) | copy-start | bytes 98308
  195.2 99.5 %copy-start.5 = (f32[256]{0:T(256)S(1)}, f32[256]{0:T(256)}, u32[]{:S(2)}) copy-start(f32[256]{0:T(256)} %param.10) | copy-start | bytes 3076
  196.8 371.9 %reduce-scatter.5.cloned.1.call-start = ((), (), s32[]{:S(2)}) async-start(), calls=%async_computation.3 | async-start | bytes 557056 | tf_op jit(solution)/shard_map/reduce_scatter | solution.py:88
  319.7 38.6 %collective-permute-start.5 = (bf16[1024,256]{1,0:T(8,128)(2,1)S(1)}, bf16[1024,256]{1,0:T(8,128)(2,1)S(1)}, u32[]{:S(2)}, u32[]{:S(2)}) collective-permute-start(bf16[1024,256]{1,0:T(8,128)(2,1)S(1)} %fusion.19), channel_id=1, source_target_pairs={{0,256},{16,272},{32,288},{48,304},{64,320},{80,336},{96,352},{112... | collective-permute-start | bytes 1572872 | tf_op jit(solution)/shard_map/ppermute | solution.py:9
  359.0 40.7 %collective-permute-start.6 = (bf16[1024,256]{1,0:T(8,128)(2,1)S(1)}, bf16[1024,256]{1,0:T(8,128)(2,1)S(1)}, u32[]{:S(2)}, u32[]{:S(2)}) collective-permute-start(bf16[1024,256]{1,0:T(8,128)(2,1)S(1)} %get-tuple-element.17), channel_id=1, source_target_pairs={{0,384},{16,400},{32,416},{48,432},{64,448},{80,464},{96,480},{112... | collective-permute-start | bytes 1572872 | tf_op jit(solution)/shard_map/ppermute | solution.py:9
  399.9 51.2 %collective-permute-start.7 = (bf16[1024,256]{1,0:T(8,128)(2,1)S(1)}, bf16[1024,256]{1,0:T(8,128)(2,1)S(1)}, u32[]{:S(2)}, u32[]{:S(2)}) collective-permute-start(bf16[1024,256]{1,0:T(8,128)(2,1)S(1)} %convert_select_fusion.2), channel_id=1, source_target_pairs={{0,448},{16,464},{32,480},{48,496},{64,0},{80,16},{96,32},{112,48}... | collective-permute-start | bytes 1572872 | tf_op jit(solution)/shard_map/ppermute | solution.py:9
  451.2 15.7 %collective-permute-start.8 = (bf16[1024,256]{1,0:T(8,128)(2,1)S(1)}, bf16[1024,256]{1,0:T(8,128)(2,1)S(1)}, u32[]{:S(2)}, u32[]{:S(2)}) collective-permute-start(bf16[1024,256]{1,0:T(8,128)(2,1)S(1)} %fusion.26), channel_id=1, source_target_pairs={{0,480},{16,496},{32,0},{48,16},{64,32},{80,48},{96,64},{112,80},{... | collective-permute-start | bytes 1572872 | tf_op jit(solution)/shard_map/ppermute | solution.py:9
  467.1 101.5 %copy-start.2 = (bf16[64,256]{1,0:T(8,128)(2,1)S(1)}, bf16[64,256]{1,0:T(8,128)(2,1)}, u32[]{:S(2)}) copy-start(bf16[64,256]{1,0:T(8,128)(2,1)} %param.8) | copy-start | bytes 98308
  467.1 14.9 %collective-permute-start.9 = (bf16[1024,256]{1,0:T(8,128)(2,1)S(1)}, bf16[1024,256]{1,0:T(8,128)(2,1)S(1)}, u32[]{:S(2)}, u32[]{:S(2)}) collective-permute-start(bf16[1024,256]{1,0:T(8,128)(2,1)S(1)} %fusion.27), channel_id=1, source_target_pairs={{0,496},{16,0},{32,16},{48,32},{64,48},{80,64},{96,80},{112,96},{1... | collective-permute-start | bytes 1572872 | tf_op jit(solution)/shard_map/ppermute | solution.py:9
  483.1 234.6 %all-reduce.3.cloned.1.call-start = ((), (), s32[]{:S(2)}) async-start(), calls=%async_computation.4 | async-start | bytes 524288 | tf_op jit(solution)/shard_map/psum | solution.py:99
  570.3 418.5 %all-reduce.5.cloned.1.call-start = ((), (), s32[]{:S(2)}) async-start(), calls=%async_computation.5 | async-start | bytes 524288 | tf_op jit(solution)/shard_map/psum | solution.py:99
Sparse Core Ops, SparseCore 0:
  196.9 97.7 reduce-scatter.2
  483.2 85.3 reduce-scatter.4
  571.5 146.0 all-reduce.2
  720.6 268.0 all-reduce.4
